TPU v7x, 128 devices: a whole 4x4x4 slice. The times are simulated.
128 devices in a mesh: expert: 32 (over y, x, core), dp: 4 (over z).
Axes of the slice: x: 4, y: 4, z: 4, core: 2. Of those that a mesh axis runs over, the one named last changes fastest.
Arguments:
- tokens: bfloat16 [8192, 3584], P(('expert', 'dp')), may hold values from -6 to 6
- out_grad: bfloat16 [8192, 3584], P(('expert', 'dp')), may hold values from -6 to 6
- route_ids: int32 [8192, 8], P(('expert', 'dp')), may hold values from 0 to 31, all different within a row; in each aligned block of 64 rows (0 to 63, 64 to 127, ...) at most 20 rows name the same one
- route_logits: float32 [8192, 8], P(('expert', 'dp')), may hold values from -6 to 6
- gate_up: bfloat16 [32, 2, 3584, 1024], P('expert', None, None, 'dp'), may hold values from -0.09375 to 0.09375
- down: bfloat16 [32, 1024, 3584], P('expert', 'dp'), may hold values from -0.1875 to 0.1875
- moment1: bfloat16 [32, 1024, 3584], P('expert', 'dp'), may hold values from -8 to 8
- moment2: bfloat16 [32, 1024, 3584], P('expert', 'dp'), may hold values from 0.5 to 20
Outputs:
- token_grad: bfloat16 [8192, 3584], P(('expert', 'dp'))
- router_grad: float32 [8192, 8], P(('expert', 'dp'))
- new_down: bfloat16 [32, 1024, 3584], P('expert', 'dp')
- new_moment1: bfloat16 [32, 1024, 3584], P('expert', 'dp')
- new_moment2: bfloat16 [32, 1024, 3584], P('expert', 'dp')
Inputs may be any that keep to these rules, and one draw needn't show every extreme that they name: `route_ids`: each row names 8 different experts. Within the 64 rows of one device no expert is named more than 20 times, and in every draw the rows of some device name some expert exactly 20 times.
All inputs are finite; a program needn't handle non-finite values.
Results may differ from a plain program's by a relative error of at most 0.012.
Values may be sent and summed in bfloat16 or wider, within the bound.
No kernel may reach another device: no remote copies, remote signals or barrier semaphores. Data moves between devices by JAX's collectives and lax.ppermute only.
A program may use at most 192 MiB of HBM per device.

v0:
```python
import jax
import jax.numpy as jnp
from jax import lax
from jax.sharding import PartitionSpec as P

STEP = 10
ROUTE_SCALE = 2.5
BETA_ONE = 0.9
BETA_TWO = 0.95
LEARN_RATE = 0.001
DECAY = 0.1
EPSILON = 1e-08
LANE = 128
HALVES = 2


def contract_last(left, right):
    return lax.dot_general(
        left, right, (((1,), (1,)), ((), ())), preferred_element_type=jnp.float32
    )


def contract_first(left, right):
    return lax.dot_general(
        left, right, (((0,), (0,)), ((), ())), preferred_element_type=jnp.float32
    )


def shards(tokens, out_grad, route_ids, route_logits, gate_up, down, moment1, moment2):
    experts = lax.axis_size("expert")
    data_ways = lax.axis_size("dp")
    tok_rows, model_width = tokens.shape
    top_count = route_ids.shape[1]
    local_ffw = down.shape[1]
    part_ffw = local_ffw // HALVES
    capacity = min(tok_rows, max(2, 5 * tok_rows * top_count // (4 * experts)))
    capacity = -(-capacity // 8) * 8
    slot_count = experts * capacity
    scores = jax.nn.sigmoid(route_logits)
    score_sum = jnp.sum(scores, axis=1, keepdims=True)
    route_weight = (ROUTE_SCALE * scores / score_sum).astype(jnp.bfloat16)
    flat_ids = route_ids.reshape(-1)
    onehot = (flat_ids[:, None] == jnp.arange(experts, dtype=jnp.int32)[None, :]).astype(jnp.int32)
    before = jnp.cumsum(onehot, axis=0) - onehot
    places = jnp.sum(before * onehot, axis=1)
    slot_index = flat_ids * capacity + places
    matched = (jnp.arange(slot_count, dtype=jnp.int32)[:, None] == slot_index[None, :]).astype(
        jnp.float32
    )
    tok_match = jnp.sum(matched.reshape(slot_count, tok_rows, top_count), axis=2).astype(
        jnp.bfloat16
    )
    send_weight = jnp.sum(matched * route_weight.astype(jnp.float32).reshape(-1)[None, :], axis=1)
    weight_block = jnp.zeros((slot_count, LANE), jnp.float32).at[:, 0].set(send_weight)
    payload = jnp.concatenate([tokens, out_grad], axis=1)
    send_rows = jnp.dot(tok_match, payload, preferred_element_type=jnp.float32)
    send_rows = jnp.concatenate([send_rows, weight_block], axis=1).astype(jnp.bfloat16)
    send_rows = send_rows.reshape(experts, capacity, 2 * model_width + LANE)
    full_down = lax.all_gather(down, "dp", axis=1, tiled=True)[0]
    gu_parts = [
        lax.all_gather(
            gate_up[:, :, :, h * part_ffw : (h + 1) * part_ffw], "dp", axis=3, tiled=True
        )[0]
        for h in range(HALVES)
    ]
    recv_rows = lax.all_to_all(send_rows, "expert", split_axis=0, concat_axis=0, tiled=True)
    recv_rows = recv_rows.reshape(slot_count, 2 * model_width + LANE)
    xs_rows = recv_rows[:, :model_width]
    gs_rows = recv_rows[:, model_width : 2 * model_width]
    slot_weight = recv_rows[:, 2 * model_width].astype(jnp.float32)
    back_full = contract_last(gs_rows, full_down)
    back_full = back_full.reshape(slot_count, data_ways, HALVES, part_ffw)
    scaled = (slot_weight[:, None] * gs_rows.astype(jnp.float32)).astype(jnp.bfloat16)
    grad_parts = []
    affinity = jnp.zeros((slot_count,), jnp.float32)
    route_acc = jnp.zeros((slot_count, model_width), jnp.float32)
    for h in range(HALVES):
        gate_w = gu_parts[h][0]
        up_w = gu_parts[h][1]
        back_raw = back_full[:, :, h, :].reshape(slot_count, data_ways * part_ffw)
        pre_gate = jnp.dot(xs_rows, gate_w, preferred_element_type=jnp.float32)
        pre_up = jnp.dot(xs_rows, up_w, preferred_element_type=jnp.float32)
        sig_gate = jax.nn.sigmoid(pre_gate)
        silu_gate = pre_gate * sig_gate
        hidden = (silu_gate * pre_up).astype(jnp.bfloat16)
        affinity = affinity + jnp.sum(hidden.astype(jnp.float32) * back_raw, axis=1)
        local_grad = contract_first(hidden, scaled)
        grad_parts.append(
            lax.psum_scatter(local_grad.astype(jnp.bfloat16), "dp", scatter_dimension=0, tiled=True)
        )
        back = slot_weight[:, None] * back_raw
        gate_grad = (back * pre_up * sig_gate * (1.0 + pre_gate * (1.0 - sig_gate))).astype(
            jnp.bfloat16
        )
        up_grad = (back * silu_gate).astype(jnp.bfloat16)
        route_acc = route_acc + contract_last(gate_grad, gate_w) + contract_last(up_grad, up_w)
    affinity_block = (
        jnp.zeros((slot_count, LANE), jnp.float32)
        .at[:, 0]
        .set(affinity.astype(jnp.bfloat16).astype(jnp.float32))
    )
    ret_rows = jnp.concatenate(
        [route_acc.astype(jnp.bfloat16).astype(jnp.float32), affinity_block], axis=1
    )
    ret_rows = ret_rows.astype(jnp.bfloat16).reshape(experts, capacity, model_width + LANE)
    back_rows = lax.all_to_all(ret_rows, "expert", split_axis=0, concat_axis=0, tiled=True)
    back_rows = back_rows.reshape(slot_count, model_width + LANE)
    token_grad = contract_first(tok_match, back_rows[:, :model_width]).astype(jnp.bfloat16)
    back_affinity = back_rows[:, model_width].astype(jnp.float32)
    route_affinity = jnp.sum(matched * back_affinity[:, None], axis=0)
    route_affinity = route_affinity.reshape(tok_rows, top_count)
    mixed = jnp.sum(route_affinity * scores, axis=1, keepdims=True) / score_sum
    router_grad = ROUTE_SCALE * scores * (1.0 - scores) * (route_affinity - mixed) / score_sum
    grad_shard = jnp.concatenate(grad_parts, axis=0).astype(jnp.float32)
    down_grad = (grad_shard / data_ways)[None]
    corr_one = 1.0 - BETA_ONE**STEP
    corr_two = 1.0 - BETA_TWO**STEP
    down_wide = down.astype(jnp.float32)
    first = BETA_ONE * moment1.astype(jnp.float32) + (1.0 - BETA_ONE) * down_grad
    second = BETA_TWO * moment2.astype(jnp.float32) + (1.0 - BETA_TWO) * down_grad * down_grad
    update = first / corr_one / (jnp.sqrt(second / corr_two) + EPSILON) + DECAY * down_wide
    new_down = (down_wide - LEARN_RATE * update).astype(jnp.bfloat16)
    return (
        token_grad,
        router_grad,
        new_down,
        first.astype(jnp.bfloat16),
        second.astype(jnp.bfloat16),
    )


def solution(mesh):
    placed = (
        P(("expert", "dp"), None),
        P(("expert", "dp"), None),
        P(("expert", "dp"), None),
        P(("expert", "dp"), None),
        P("expert", None, None, "dp"),
        P("expert", "dp", None),
        P("expert", "dp", None),
        P("expert", "dp", None),
    )
    return jax.shard_map(
        shards,
        mesh=mesh,
        in_specs=placed,
        out_specs=(
            P(("expert", "dp"), None),
            P(("expert", "dp"), None),
            P("expert", "dp", None),
            P("expert", "dp", None),
            P("expert", "dp", None),
        ),
        check_vma=False,
    )
```

profile of v0, /device:TPU:1, one launch (start us, length us, event | category | flops | bytes accessed | tf_op | source)
XLA Modules:
  0.0 411.3 jit_solution(7383616715635387772)
XLA Ops:
  7.2 0.0 all-gather.4.cloned.1.call-start
  7.2 0.7 all-gather.4.cloned.1.call-update
  7.9 0.0 all-gather.8.cloned.1.call-start
  8.0 4.2 %fusion.43 = (bf16[1,2,3584,128]{3,2,1,0:T(8,128)(2,1)}, bf16[1,2,3584,128]{3,2,1,0:T(8,128)(2,1)}) fusion(bf16[1,2,3584,256]{3,2,1,0:T(8,128)(2,1)} %param.16), kind=kLoop, calls=%fused_computation.92 | loop fusion | bytes 7340032 | tf_op jit(solution)/shard_map/slice | solution.py:62
  12.2 0.0 all-gather.8.cloned.1.call-update
  12.2 0.1 copy.42
  12.3 0.1 eq.50
  12.4 0.1 eq.46
  12.5 1.2 reduce-window.6
  13.7 0.2 slice_reduce_fusion
  14.0 0.1 copy.47
  14.1 0.1 reshape.225
  14.2 0.1 fusion.36
  14.3 0.1 reduce_sum.75
  14.4 0.6 compare_reduce_fusion
  15.0 0.2 select_reduce_fusion.1
  15.3 0.7 select_convert_fusion.1
  15.9 0.2 reshape.230
  16.1 0.1 copy.45
  16.2 0.1 copy.46
  16.3 0.5 convert_reduce_fusion
  16.8 0.0 copy-done.4
  16.8 0.0 copy-done.5
  16.9 3.3 convolution_convert_fusion
  20.1 5.0 %pad_maximum_fusion = bf16[32,24,7296]{2,1,0:T(8,128)(2,1)} fusion(bf16[32,24,128]{2,1,0:T(8,128)(2,1)S(1)} %bitcast.86, bf16[32,24,7168]{2,1,0:T(8,128)(2,1)S(1)} %bitcast.80), kind=kLoop, calls=%fused_computation.1 | loop fusion | flops 22413312 | bytes 22413312 | tf_op jit(solution)/shard_map/concatenate | solution.py:57
  25.1 8.6 %all-to-all-start = ((bf16[32,24,7296]{2,1,0:T(8,128)(2,1)}), bf16[32,24,7296]{2,1,0:T(8,128)(2,1)}, u32[]{:S(2)}, u32[]{:S(2)}) async-start(bf16[32,24,7296]{2,1,0:T(8,128)(2,1)} %pad_maximum_fusion), calls=%async_computation | async-start | bytes 22413312 | tf_op jit(solution)/shard_map/all_to_all | solution.py:66
  33.8 0.0 all-gather.6.cloned.1.call-start
  33.8 0.7 all-gather.6.cloned.1.call-update
  34.5 0.2 reduce-scatter.5.cloned.1.call-start
  34.7 134.1 %all-to-all-done = bf16[32,24,7296]{2,1,0:T(8,128)(2,1)} async-done(((bf16[32,24,7296]{2,1,0:T(8,128)(2,1)}), bf16[32,24,7296]{2,1,0:T(8,128)(2,1)}, u32[]{:S(2)}, u32[]{:S(2)}) %all-to-all-start) | async-done | bytes 11206688 | tf_op jit(solution)/shard_map/all_to_all | solution.py:66
  168.8 1.1 convert_reduce_fusion.2
  169.9 0.0 all-gather.4.cloned.1.call-done
  169.9 9.8 %fusion.2 = f32[768,4,2,128]{0,3,2,1:T(8,128)S(1)} fusion(bf16[4,2,128,3584]{3,2,1,0:T(8,128)(2,1)} %bitcast.88, bf16[768,7296]{1,0:T(8,128)(2,1)} %bitcast.3), kind=kOutput, calls=%fused_computation.9 | convolution fusion | flops 5637144576 | bytes 15990784 | tf_op jit(solution)/shard_map/dot_general | solution.py:18
  179.7 0.3 fusion.44
  180.0 0.0 all-gather.8.cloned.1.call-done
  180.1 0.0 copy-start.2
  180.1 7.8 %fusion.14 = f32[768,512]{0,1:T(8,128)S(1)} fusion(bf16[768,7296]{1,0:T(8,128)(2,1)} %bitcast.3, bf16[1,2,3584,512]{3,2,1,0:T(8,128)(2,1)} %all-gather.8.cloned.1.call-done), kind=kOutput, calls=%fused_computation.28 | convolution fusion | flops 2818572288 | bytes 10747904 | tf_op jit(solution)/shard_map/dot_general | solution.py:81
  188.0 7.7 %fusion.27 = (f32[768]{0:T(1024)S(1)}, bf16[768,512]{0,1:T(8,128)(2,1)S(1)}, bf16[768,512]{0,1:T(8,128)(2,1)}, bf16[768,512]{0,1:T(8,128)(2,1)}) fusion(f32[768,4,1,128]{0,3,2,1:T(8,128)S(1)} %get-tuple-element.57, f32[768,512]{0,1:T(8,128)S(1)} %fusion.14, f32[768]{0:T(1024)S(1)} %convert_reduce_fusion.2, bf16[1,2,3584,512]{3,2,1,0:T(8,128)(2,1)S(1)} %copy-done.2, ...), kind=kOutput, calls=%fused_computation.44 | convolution fusion | flops 2826042624 | bytes 14687232 | tf_op jit(solution)/shard_map/dot_general | solution.py:82
  195.6 7.5 %convolution_convert_fusion.1 = bf16[512,3584]{1,0:T(8,128)(2,1)} fusion(bf16[768,512]{0,1:T(8,128)(2,1)S(1)} %get-tuple-element.45, f32[768]{0:T(1024)S(1)} %convert_reduce_fusion.2, bf16[768,7296]{1,0:T(8,128)(2,1)} %bitcast.3), kind=kOutput, calls=%fused_computation.4 | convolution fusion | flops 2828664832 | bytes 9964544 | tf_op jit(solution)/shard_map/dot_general | solution.py:24
  203.2 0.0 reduce-scatter.5.cloned.1.call-update
  203.2 0.3 reduce-scatter.3.cloned.1.call-start
  203.5 44.5 %all-gather.6.cloned.1.call-done = bf16[1,2,3584,512]{3,2,1,0:T(8,128)(2,1)} async-done(((bf16[1,2,3584,128]{3,2,1,0:T(8,128)(2,1)}), bf16[1,2,3584,512]{3,2,1,0:T(8,128)(2,1)}) %all-gather.6.cloned.1.call-update) | async-done | bytes 7340048 | tf_op jit(solution)/shard_map/all_gather | solution.py:61
  248.0 6.9 %fusion.18 = f32[768,512]{0,1:T(8,128)S(1)} fusion(bf16[768,7296]{1,0:T(8,128)(2,1)} %bitcast.3, bf16[1,2,3584,512]{3,2,1,0:T(8,128)(2,1)} %all-gather.6.cloned.1.call-done), kind=kOutput, calls=%fused_computation.32 | convolution fusion | flops 2818572288 | bytes 10747904 | tf_op jit(solution)/shard_map/dot_general | solution.py:81
  254.9 7.6 %fusion.28 = (f32[768]{0:T(1024)S(1)}, bf16[768,512]{0,1:T(8,128)(2,1)S(1)}, bf16[768,512]{0,1:T(8,128)(2,1)}, bf16[768,512]{0,1:T(8,128)(2,1)}) fusion(f32[768,4,1,128]{0,3,2,1:T(8,128)S(1)} %get-tuple-element.58, f32[768,512]{0,1:T(8,128)S(1)} %fusion.18, f32[768]{0:T(1024)S(1)} %convert_reduce_fusion.2, bf16[1,2,3584,512]{3,2,1,0:T(8,128)(2,1)S(1)} %copy-done.8, ...), kind=kOutput, calls=%fused_computation.47 | convolution fusion | flops 2826042624 | bytes 14687232 | tf_op jit(solution)/shard_map/dot_general | solution.py:82
  262.5 7.5 %convolution_convert_fusion.2 = bf16[512,3584]{1,0:T(8,128)(2,1)} fusion(bf16[768,512]{0,1:T(8,128)(2,1)S(1)} %get-tuple-element.47, f32[768]{0:T(1024)S(1)} %convert_reduce_fusion.2, bf16[768,7296]{1,0:T(8,128)(2,1)} %bitcast.3), kind=kOutput, calls=%fused_computation.5 | convolution fusion | flops 2828664832 | bytes 9964544 | tf_op jit(solution)/shard_map/dot_general | solution.py:24
  270.0 0.0 reduce-scatter.3.cloned.1.call-update
  270.1 1.1 copy-done.9
  271.2 8.2 %fusion.24 = f32[768,3584]{1,0:T(8,128)} fusion(bf16[768,512]{0,1:T(8,128)(2,1)S(1)} %copy-done.9, bf16[1,2,3584,512]{3,2,1,0:T(8,128)(2,1)} %all-gather.8.cloned.1.call-done), kind=kOutput, calls=%fused_computation.38 | convolution fusion | flops 2818572288 | bytes 15466496 | tf_op jit(solution)/shard_map/dot_general | solution.py:18
  279.3 8.1 %fusion.22 = f32[768,3584]{1,0:T(8,128)} fusion(bf16[768,512]{0,1:T(8,128)(2,1)S(1)} %copy-done.11, bf16[1,2,3584,512]{3,2,1,0:T(8,128)(2,1)} %all-gather.6.cloned.1.call-done), kind=kOutput, calls=%fused_computation.36 | convolution fusion | flops 2818572288 | bytes 15466496 | tf_op jit(solution)/shard_map/dot_general | solution.py:18
  287.4 5.8 %fusion.23 = f32[768,3584]{1,0:T(8,128)} fusion(bf16[768,512]{0,1:T(8,128)(2,1)S(1)} %copy-done.10, bf16[1,2,3584,512]{3,2,1,0:T(8,128)(2,1)S(1)} %bitcast.90), kind=kOutput, calls=%fused_computation.37 | convolution fusion | flops 2818572288 | bytes 15466496 | tf_op jit(solution)/shard_map/dot_general | solution.py:18
  293.2 15.9 %add_convert_fusion = bf16[768,3584]{1,0:T(8,128)(2,1)} fusion(f32[768,3584]{1,0:T(8,128)} %fusion.24, f32[768,3584]{1,0:T(8,128)} %fusion.23, f32[768,3584]{1,0:T(8,128)} %fusion.22, bf16[768,512]{0,1:T(8,128)(2,1)S(1)} %copy-done.3, bf16[1,2,3584,512]{3,2,1,0:T(8,128)(2,1)} %all-gather.8.cloned.1.call-done), kind=kOutput, calls=%fused_computation.3 | convolution fusion | flops 2829582336 | bytes 42991616 | tf_op jit(solution)/shard_map/dot_general | solution.py:18
  309.2 0.6 select_convert_fusion
  309.8 0.2 reshape.232
  310.1 3.0 pad_maximum_fusion.1
  313.0 75.7 %all_to_all.10 = bf16[32,24,3712]{2,1,0:T(8,128)(2,1)S(1)} all-to-all(bf16[32,24,3712]{2,1,0:T(8,128)(2,1)S(1)} %pad_maximum_fusion.1), channel_id=1, replica_groups=mesh['expert'=32,'dp'=4] {'expert'}, dimensions={0} | all-to-all | bytes 11403264 | tf_op jit(solution)/shard_map/all_to_all | solution.py:106
  388.8 2.5 copy-done.1
  391.3 0.1 convert_reduce_fusion.1
  391.5 0.3 select_reduce_fusion
  391.7 0.1 reshape.224
  391.8 0.1 copy.51
  391.9 0.6 multiply_divide_fusion
  392.6 4.4 %fusion.5 = bf16[64,3584]{1,0:T(8,128)(2,1)} fusion(bf16[768,3712]{1,0:T(8,128)(2,1)} %bitcast.83, bf16[768,64]{0,1:T(8,128)(2,1)S(1)} %convert_reduce_fusion), kind=kOutput, calls=%fused_computation.15 | convolution fusion | flops 352550912 | bytes 6062080 | tf_op jit(solution)/shard_map/dot_general | solution.py:24
  397.0 0.0 copy-done
  397.0 7.8 %fusion.26 = (bf16[1,256,3584]{2,1,0:T(8,128)(2,1)}, bf16[1,256,3584]{2,1,0:T(8,128)(2,1)}, bf16[1,256,3584]{2,1,0:T(8,128)(2,1)}) fusion(bf16[1,256,3584]{2,1,0:T(8,128)(2,1)} %param.19, bf16[1,128,3584]{2,1,0:T(8,128)(2,1)} %bitcast.84, bf16[1,128,3584]{2,1,0:T(8,128)(2,1)} %bitcast.85, bf16[1,256,3584]{2,1,0:T(8,128)(2,1)} %param.18, ...), kind=kLoop, calls=%fused_computation.40 | loop fusion | flops 23855104 | bytes 12845056 | tf_op jit(solution)/shard_map/convert_element_type | solution.py:128
  (36 shorter events, 0.3 us)
Async XLA Ops:
  7.2 162.7 %all-gather.4.cloned.1.call-start = ((), (), s32[]{:S(2)}) async-start(), calls=%async_computation.4 | async-start | bytes 9175040 | tf_op jit(solution)/shard_map/all_gather | solution.py:59
  7.9 4.3 %copy-start.7 = (s32[64,8]{0,1:T(8,128)S(1)}, s32[64,8]{0,1:T(8,128)}, u32[]{:S(2)}) copy-start(s32[64,8]{0,1:T(8,128)} %param.14) | copy-start | bytes 6148
  7.9 6.0 %copy-start.6 = (f32[64,8]{0,1:T(8,128)S(1)}, f32[64,8]{0,1:T(8,128)}, u32[]{:S(2)}) copy-start(f32[64,8]{0,1:T(8,128)} %param.15) | copy-start | bytes 6148
  7.9 8.9 %copy-start.4 = (bf16[64,3584]{1,0:T(8,128)(2,1)S(1)}, bf16[64,3584]{1,0:T(8,128)(2,1)}, u32[]{:S(2)}) copy-start(bf16[64,3584]{1,0:T(8,128)(2,1)} %param.13) | copy-start | bytes 1376260
  7.9 8.9 %copy-start.5 = (bf16[64,3584]{1,0:T(8,128)(2,1)S(1)}, bf16[64,3584]{1,0:T(8,128)(2,1)}, u32[]{:S(2)}) copy-start(bf16[64,3584]{1,0:T(8,128)(2,1)} %param.12) | copy-start | bytes 1376260
  7.9 172.1 %all-gather.8.cloned.1.call-start = ((), (), s32[]{:S(2)}) async-start(), calls=%async_computation.6 | async-start | bytes 9175040 | tf_op jit(solution)/shard_map/all_gather | solution.py:61
  25.1 143.7 %all-to-all-start = ((bf16[32,24,7296]{2,1,0:T(8,128)(2,1)}), bf16[32,24,7296]{2,1,0:T(8,128)(2,1)}, u32[]{:S(2)}, u32[]{:S(2)}) async-start(bf16[32,24,7296]{2,1,0:T(8,128)(2,1)} %pad_maximum_fusion), calls=%async_computation | async-start | bytes 22413312 | tf_op jit(solution)/shard_map/all_to_all | solution.py:66
  33.8 214.2 %all-gather.6.cloned.1.call-start = ((), (), s32[]{:S(2)}) async-start(), calls=%async_computation.5 | async-start | bytes 9175040 | tf_op jit(solution)/shard_map/all_gather | solution.py:61
  34.5 362.5 %reduce-scatter.5.cloned.1.call-start = ((), (), s32[]{:S(2)}) async-start(), calls=%async_computation.8 | async-start | bytes 4587520 | tf_op jit(solution)/shard_map/reduce_scatter | solution.py:89
  180.1 7.9 %copy-start.2 = (bf16[1,2,3584,512]{3,2,1,0:T(8,128)(2,1)S(1)}, bf16[1,2,3584,512]{3,2,1,0:T(8,128)(2,1)}, u32[]{:S(2)}) copy-start(bf16[1,2,3584,512]{3,2,1,0:T(8,128)(2,1)} %all-gather.8.cloned.1.call-done) | copy-start | bytes 22020100
  203.2 193.8 %reduce-scatter.3.cloned.1.call-start = ((), (), s32[]{:S(2)}) async-start(), calls=%async_computation.7 | async-start | bytes 4587520 | tf_op jit(solution)/shard_map/reduce_scatter | solution.py:89
  248.0 6.9 %copy-start.8 = (bf16[1,2,3584,512]{3,2,1,0:T(8,128)(2,1)S(1)}, bf16[1,2,3584,512]{3,2,1,0:T(8,128)(2,1)}, u32[]{:S(2)}) copy-start(bf16[1,2,3584,512]{3,2,1,0:T(8,128)(2,1)} %all-gather.6.cloned.1.call-done) | copy-start | bytes 22020100
  270.0 1.1 copy-start.9
  271.2 8.2 %copy-start.11 = (bf16[768,512]{0,1:T(8,128)(2,1)S(1)}, bf16[768,512]{0,1:T(8,128)(2,1)}, u32[]{:S(2)}) copy-start(bf16[768,512]{0,1:T(8,128)(2,1)} %get-tuple-element.56) | copy-start | bytes 2359300
  271.2 16.2 %slice-start = ((s8[7340032]{0:T(1024)(128)(4,1)}), s8[4194304]{0:T(1024)(128)(4,1)S(1)}, s32[]{:S(2)}) async-start(s8[7340032]{0:T(1024)(128)(4,1)} %bitcast.89), calls=%async_computation.9 | async-start | bytes 8388608
  279.3 8.1 %slice-start.1 = ((s8[7340032]{0:T(1024)(128)(4,1)}), s8[3145728]{0:T(1024)(128)(4,1)S(1)}, s32[]{:S(2)}) async-start(s8[7340032]{0:T(1024)(128)(4,1)} %bitcast.89), calls=%async_computation.10 | async-start | bytes 6291456
  279.3 8.1 %copy-start.10 = (bf16[768,512]{0,1:T(8,128)(2,1)S(1)}, bf16[768,512]{0,1:T(8,128)(2,1)}, u32[]{:S(2)}) copy-start(bf16[768,512]{0,1:T(8,128)(2,1)} %get-tuple-element.48) | copy-start | bytes 2359300
  287.4 5.8 %copy-start.3 = (bf16[768,512]{0,1:T(8,128)(2,1)S(1)}, bf16[768,512]{0,1:T(8,128)(2,1)}, u32[]{:S(2)}) copy-start(bf16[768,512]{0,1:T(8,128)(2,1)} %get-tuple-element.55) | copy-start | bytes 2359300
  388.8 2.6 copy-start.1
  388.8 8.2 %copy-start = (bf16[1,256,3584]{2,1,0:T(8,128)(2,1)S(1)}, bf16[1,256,3584]{2,1,0:T(8,128)(2,1)}, u32[]{:S(2)}) copy-start(bf16[1,256,3584]{2,1,0:T(8,128)(2,1)} %param.17) | copy-start | bytes 5505028
Sparse Core Ops, SparseCore 0:
  9.6 77.5 all-gather.3
  89.5 77.6 all-gather.7
  169.4 78.5 all-gather.5
  250.3 44.3 reduce-scatter.4
  297.0 42.3 reduce-scatter.2
where the time goes:
time: 412 us; the launch traced here: 411 us
  waiting for transfers between devices  180 us (44%)
  matrix products  101 us (25%)
  blocking collectives  75.7 us (18%)
  other arithmetic  22 us (5%)
  between operations  14.1 us (3%)
  local copies, waits for them, and re-layouts  9.74 us (2%)
  starting transfers between devices  9.23 us (2%)
    all_to_all x1, waiting for transfers between devices, shards(): lax.all_to_all(send_rows, 'expert', split_axis=0, concat_axis=0, tiled=True)  134 us
    all_to_all x1, blocking collectives, shards(): lax.all_to_all(ret_rows, 'expert', split_axis=0, concat_axis=0, tiled=True)  75.7 us
    dot_general x5, matrix products, contract_last(): lax.dot_general(left, right, (((1,), (1,)), ((), ())), preferred_element_...  47.8 us
    all_gather x2, waiting for transfers between devices, shards(): lax.all_gather(gate_up[:, :, :, h * part_ffw:(h + 1) * part_ffw], 'dp', a...  44.5 us
    dot_general x3, matrix products, contract_first(): lax.dot_general(left, right, (((0,), (0,)), ((), ())), preferred_element_...  19.4 us
    dot_general x2, matrix products, shards(): pre_up = jnp.dot(xs_rows, up_w, preferred_element_type=jnp.float32)  15.3 us
    dot_general x2, matrix products, shards(): pre_gate = jnp.dot(xs_rows, gate_w, preferred_element_type=jnp.float32)  14.8 us
    all_to_all x1, starting transfers between devices, shards(): lax.all_to_all(send_rows, 'expert', split_axis=0, concat_axis=0, tiled=True)  8.63 us
  transfers between devices with their start and end apart: 6, of which 2 were waited for; matrix products, arithmetic and copies ran while one was open for 29% of the time, Pallas kernels for 0%

commit v1 on v0

--- a/solution.py
+++ b/solution.py
@@ -12,6 +12,24 @@
 EPSILON = 1e-08
 LANE = 128
 HALVES = 2
+
+
+def ring_gather(shard, axis, dim):
+    ways, here, step = (lax.axis_size(axis), lax.axis_index(axis), shard.shape[dim])
+    shape = [n * ways if d == dim else n for d, n in enumerate(shard.shape)]
+    full = lax.dynamic_update_slice_in_dim(
+        jnp.zeros(shape, shard.dtype), shard, here * step, axis=dim
+    )
+    going_up = going_down = shard
+    for far in range(1, ways // 2 + 1):
+        going_up = lax.ppermute(going_up, axis, [(d, (d + 1) % ways) for d in range(ways)])
+        full = lax.dynamic_update_slice_in_dim(full, going_up, (here - far) % ways * step, axis=dim)
+        if 2 * far < ways:
+            going_down = lax.ppermute(going_down, axis, [(d, (d - 1) % ways) for d in range(ways)])
+            full = lax.dynamic_update_slice_in_dim(
+                full, going_down, (here + far) % ways * step, axis=dim
+            )
+    return full
 
 
 def contract_last(left, right):
@@ -58,9 +76,7 @@
     send_rows = send_rows.reshape(experts, capacity, 2 * model_width + LANE)
     full_down = lax.all_gather(down, "dp", axis=1, tiled=True)[0]
     gu_parts = [
-        lax.all_gather(
-            gate_up[:, :, :, h * part_ffw : (h + 1) * part_ffw], "dp", axis=3, tiled=True
-        )[0]
+        ring_gather(gate_up[:, :, :, h * part_ffw : (h + 1) * part_ffw], "dp", 3)[0]
         for h in range(HALVES)
     ]
     recv_rows = lax.all_to_all(send_rows, "expert", split_axis=0, concat_axis=0, tiled=True)

time: 412 us -> 433 us (1.051); the launches traced: 411 us -> 426 us
  local copies, waits for them, and re-layouts: 9.74 us -> 33.4 us
  waiting for transfers between devices: 180 us -> 163 us
  starting transfers between devices: 9.23 us -> 15.9 us
    ppermute x0 -> x6, waiting for transfers between devices: none -> 162 us  [the longest x4 162 us: ring_gather(): lax.ppermute(going_up, axis, [(d, (d + 1) % ways) for d in range(ways)])]
    all_to_all x1, waiting for transfers between devices: 134 us -> 0.01 us  [shards(): lax.all_to_all(send_rows, 'expert', split_axis=0, concat_axis=0, tiled=True)]
    all_gather x2 -> x0, waiting for transfers between devices: 44.5 us -> none  [shards(): lax.all_gather(gate_up[:, :, :, h * part_ffw:(h + 1) * part_ffw], 'dp', a...]
    dynamic_update_slice x0 -> x8, local copies, waits for them, and re-layouts: none -> 18 us  [the longest x4 10.3 us: ring_gather(): lax.dynamic_update_slice_in_dim(full, going_up, (here - far) % ways * ste...]
    ppermute x0 -> x6, starting transfers between devices: none -> 6.95 us  [the longest x2 4.8 us: ring_gather(): lax.ppermute(going_down, axis, [(d, (d - 1) % ways) for d in range(ways)])]
    squeeze x0 -> x2, local copies, waits for them, and re-layouts: none -> 4.61 us  [shards(): ring_gather(gate_up[:, :, :, h * part_ffw:(h + 1) * part_ffw], 'dp', 3)[0]]
  transfers between devices with their start and end apart: 6 -> 10, of which waited for: 2 -> 3; matrix products, arithmetic and copies ran while one was open for 29% -> 30% of each run, Pallas kernels for 0% -> 0%
where the time goes in v1:
time: 433 us; the launch traced here: 426 us
  waiting for transfers between devices  163 us (38%)
  matrix products  101 us (23%)
  blocking collectives  74.9 us (17%)
  local copies, waits for them, and re-layouts  33.4 us (8%)
  other arithmetic  23.9 us (6%)
  starting transfers between devices  15.9 us (4%)
  between operations  14.2 us (3%)
    ppermute x4, waiting for transfers between devices, ring_gather(): lax.ppermute(going_up, axis, [(d, (d + 1) % ways) for d in range(ways)])  162 us
    all_to_all x1, blocking collectives, shards(): lax.all_to_all(ret_rows, 'expert', split_axis=0, concat_axis=0, tiled=True)  74.9 us
    dot_general x5, matrix products, contract_last(): lax.dot_general(left, right, (((1,), (1,)), ((), ())), preferred_element_...  46.1 us
    dot_general x3, matrix products, contract_first(): lax.dot_general(left, right, (((0,), (0,)), ((), ())), preferred_element_...  19.6 us
    dot_general x2, matrix products, shards(): pre_gate = jnp.dot(xs_rows, gate_w, preferred_element_type=jnp.float32)  15.4 us
    dot_general x2, matrix products, shards(): pre_up = jnp.dot(xs_rows, up_w, preferred_element_type=jnp.float32)  15.1 us
    dynamic_update_slice x4, local copies, waits for them, and re-layouts, ring_gather(): lax.dynamic_update_slice_in_dim(full, going_up, (here - far) % ways * ste...  10.3 us
  transfers between devices with their start and end apart: 10, of which 3 were waited for; matrix products, arithmetic and copies ran while one was open for 30% of the time, Pallas kernels for 0%

profile of v1, /device:TPU:1, one launch (start us, length us, event | category | flops | bytes accessed | tf_op | source)
XLA Modules:
  0.0 426.1 jit_solution(13890575310525948265)
XLA Ops:
  7.2 0.8 copy.42
  7.9 0.1 eq.57
  8.0 0.1 eq.53
  8.1 0.6 compare_reduce_fusion
  8.8 1.2 reduce-window.6
  9.9 0.2 slice_reduce_fusion
  10.2 0.1 fusion.36
  10.4 0.7 fusion.42
  11.1 0.7 fusion.40
  11.9 0.1 reshape.233
  12.0 0.2 select_reduce_fusion.1
  12.3 0.7 select_convert_fusion.1
  12.9 0.2 reshape.238
  13.2 0.7 multiply_add_fusion
  13.9 0.5 convert_reduce_fusion
  14.5 4.5 %convolution_convert_fusion = bf16[768,7168]{1,0:T(8,128)(2,1)S(1)} fusion(bf16[64,3584]{1,0:T(8,128)(2,1)} %param.13, bf16[64,3584]{1,0:T(8,128)(2,1)} %param.12, bf16[768,64]{0,1:T(8,128)(2,1)S(1)} %convert_reduce_fusion), kind=kOutput, calls=%fused_computation | convolution fusion | flops 711983104 | bytes 12025856 | tf_op jit(solution)/shard_map/dot_general | solution.py:74
  19.0 4.8 %pad_maximum_fusion = bf16[32,24,7296]{2,1,0:T(8,128)(2,1)} fusion(bf16[32,24,128]{2,1,0:T(8,128)(2,1)S(1)} %bitcast.102, bf16[32,24,7168]{2,1,0:T(8,128)(2,1)S(1)} %bitcast.96), kind=kLoop, calls=%fused_computation.1 | loop fusion | flops 22413312 | bytes 22413312 | tf_op jit(solution)/shard_map/concatenate | solution.py:75
  23.8 8.6 %all-to-all-start = ((bf16[32,24,7296]{2,1,0:T(8,128)(2,1)}), bf16[32,24,7296]{2,1,0:T(8,128)(2,1)}, u32[]{:S(2)}, u32[]{:S(2)}) async-start(bf16[32,24,7296]{2,1,0:T(8,128)(2,1)} %pad_maximum_fusion), calls=%async_computation | async-start | bytes 22413312 | tf_op jit(solution)/shard_map/all_to_all | solution.py:82
  32.5 0.7 all-gather.2.cloned.1.call-update
  33.2 3.5 fusion.43
  36.8 1.6 collective-permute-start.3
  38.4 2.1 collective-permute-start.4
  40.5 2.7 collective-permute-start.1
  43.2 4.1 squeeze.35.clone.1
  47.3 1.5 bitcast_dynamic-update-slice_fusion.3
  48.8 0.5 squeeze.35.clone
  49.3 0.4 bitcast_dynamic-update-slice_fusion.7
  49.7 59.5 %collective-permute-done.3 = bf16[1,2,3584,128]{3,2,1,0:T(8,128)(2,1)} collective-permute-done((bf16[1,2,3584,128]{3,2,1,0:T(8,128)(2,1)}, bf16[1,2,3584,128]{3,2,1,0:T(8,128)(2,1)}, u32[]{:S(2)}, u32[]{:S(2)}) %collective-permute-start.3) | collective-permute-done | bytes 1835040 | tf_op jit(solution)/shard_map/ppermute | solution.py:25
  109.2 70.0 %collective-permute-done = bf16[1,2,3584,128]{3,2,1,0:T(8,128)(2,1)} collective-permute-done((bf16[1,2,3584,128]{3,2,1,0:T(8,128)(2,1)S(1)}, bf16[1,2,3584,128]{3,2,1,0:T(8,128)(2,1)}, u32[]{:S(2)}, u32[]{:S(2)}) %collective-permute-start) | collective-permute-done | bytes 1835040 | tf_op jit(solution)/shard_map/ppermute | solution.py:25
  179.2 0.5 collective-permute-start.2
  179.7 3.0 bitcast_dynamic-update-slice_fusion.2
  182.7 2.9 bitcast_dynamic-update-slice_fusion.1
  185.6 32.8 %collective-permute-done.5 = bf16[1,2,3584,128]{3,2,1,0:T(8,128)(2,1)S(1)} collective-permute-done((bf16[1,2,3584,128]{3,2,1,0:T(8,128)(2,1)}, bf16[1,2,3584,128]{3,2,1,0:T(8,128)(2,1)S(1)}, u32[]{:S(2)}, u32[]{:S(2)}) %collective-permute-start.5) | collective-permute-done | bytes 1835040 | tf_op jit(solution)/shard_map/ppermute | solution.py:25
  218.4 1.4 bitcast_dynamic-update-slice_fusion
  219.8 1.1 convert_reduce_fusion.2
  220.9 7.9 %fusion.14 = f32[768,512]{0,1:T(8,128)} fusion(bf16[768,7296]{1,0:T(8,128)(2,1)} %bitcast.3, bf16[2,3584,512]{2,1,0:T(8,128)(2,1)} %bitcast_dynamic-update-slice_fusion), kind=kOutput, calls=%fused_computation.28 | convolution fusion | flops 2818572288 | bytes 10747904 | tf_op jit(solution)/shard_map/dot_general | solution.py:97
  228.8 9.8 %fusion.2 = f32[768,4,2,128]{0,3,2,1:T(8,128)S(1)} fusion(bf16[4,2,128,3584]{3,2,1,0:T(8,128)(2,1)} %bitcast.104, bf16[768,7296]{1,0:T(8,128)(2,1)} %bitcast.3), kind=kOutput, calls=%fused_computation.9 | convolution fusion | flops 5637144576 | bytes 15990784 | tf_op jit(solution)/shard_map/dot_general | solution.py:36
  238.6 0.2 fusion.44
  238.8 1.2 copy-done.8
  240.0 8.6 %fusion.27 = (f32[768]{0:T(1024)S(1)}, bf16[768,512]{0,1:T(8,128)(2,1)S(1)}, bf16[768,512]{0,1:T(8,128)(2,1)}, bf16[768,512]{0,1:T(8,128)(2,1)}) fusion(f32[768,4,1,128]{0,3,2,1:T(8,128)S(1)} %get-tuple-element.57, f32[768,512]{0,1:T(8,128)S(1)} %copy-done.8, f32[768]{0:T(1024)S(1)} %convert_reduce_fusion.2, ...), kind=kOutput, calls=%fused_computation.52 | convolution fusion | flops 2826042624 | bytes 14686208 | tf_op jit(solution)/shard_map/dot_general | solution.py:98
  248.6 7.6 %convolution_convert_fusion.1 = bf16[512,3584]{1,0:T(8,128)(2,1)} fusion(bf16[768,512]{0,1:T(8,128)(2,1)S(1)} %get-tuple-element.45, f32[768]{0:T(1024)S(1)} %convert_reduce_fusion.2, bf16[768,7296]{1,0:T(8,128)(2,1)} %bitcast.3), kind=kOutput, calls=%fused_computation.4 | convolution fusion | flops 2828664832 | bytes 9964544 | tf_op jit(solution)/shard_map/dot_general | solution.py:42
  256.2 0.2 reduce-scatter.3.cloned.1.call-start
  256.4 3.0 bitcast_dynamic-update-slice_fusion.6
  259.4 3.0 bitcast_dynamic-update-slice_fusion.5
  262.4 2.9 bitcast_dynamic-update-slice_fusion.4
  265.3 7.6 %fusion.18 = f32[768,512]{0,1:T(8,128)S(1)} fusion(bf16[768,7296]{1,0:T(8,128)(2,1)} %bitcast.3, bf16[2,3584,512]{2,1,0:T(8,128)(2,1)} %bitcast_dynamic-update-slice_fusion.4), kind=kOutput, calls=%fused_computation.32 | convolution fusion | flops 2818572288 | bytes 10747904 | tf_op jit(solution)/shard_map/dot_general | solution.py:97
  272.9 6.5 %fusion.28 = (f32[768]{0:T(1024)S(1)}, bf16[768,512]{0,1:T(8,128)(2,1)S(1)}, bf16[768,512]{0,1:T(8,128)(2,1)S(1)}, bf16[768,512]{0,1:T(8,128)(2,1)S(1)}) fusion(f32[768,4,1,128]{0,3,2,1:T(8,128)S(1)} %get-tuple-element.58, f32[768,512]{0,1:T(8,128)S(1)} %fusion.18, f32[768]{0:T(1024)S(1)} %convert_reduce_fusion.2, bf16[2,3584,512]{2,1,0:T(8,128)(2,1)S(1)} %copy-done.3, ...), kind=kOutput, calls=%fused_computation.55 | convolution fusion | flops 2826042624 | bytes 14687232 | tf_op jit(solution)/shard_map/dot_general | solution.py:98
  279.4 6.0 %fusion.22 = f32[768,3584]{1,0:T(8,128)} fusion(bf16[768,512]{0,1:T(8,128)(2,1)S(1)} %get-tuple-element.56, bf16[2,3584,512]{2,1,0:T(8,128)(2,1)S(1)} %copy-done.3), kind=kOutput, calls=%fused_computation.36 | convolution fusion | flops 2818572288 | bytes 15466496 | tf_op jit(solution)/shard_map/dot_general | solution.py:36
  285.4 5.8 %fusion.23 = f32[768,3584]{1,0:T(8,128)} fusion(bf16[768,512]{0,1:T(8,128)(2,1)S(1)} %get-tuple-element.48, bf16[2,3584,512]{2,1,0:T(8,128)(2,1)S(1)} %copy-done.3), kind=kOutput, calls=%fused_computation.37 | convolution fusion | flops 2818572288 | bytes 15466496 | tf_op jit(solution)/shard_map/dot_general | solution.py:36
  291.1 7.9 %fusion.24 = f32[768,3584]{1,0:T(8,128)} fusion(bf16[768,512]{0,1:T(8,128)(2,1)S(1)} %copy-done.7, bf16[2,3584,512]{2,1,0:T(8,128)(2,1)} %bitcast_dynamic-update-slice_fusion), kind=kOutput, calls=%fused_computation.38 | convolution fusion | flops 2818572288 | bytes 15466496 | tf_op jit(solution)/shard_map/dot_general | solution.py:36
  299.0 7.6 %convolution_convert_fusion.2 = bf16[512,3584]{1,0:T(8,128)(2,1)} fusion(bf16[768,512]{0,1:T(8,128)(2,1)S(1)} %get-tuple-element.47, f32[768]{0:T(1024)S(1)} %convert_reduce_fusion.2, bf16[768,7296]{1,0:T(8,128)(2,1)} %bitcast.3), kind=kOutput, calls=%fused_computation.5 | convolution fusion | flops 2828664832 | bytes 9964544 | tf_op jit(solution)/shard_map/dot_general | solution.py:42
  306.7 1.1 copy-done.5
  307.8 16.7 %add_convert_fusion = bf16[768,3584]{1,0:T(8,128)(2,1)} fusion(f32[768,3584]{1,0:T(8,128)} %fusion.24, f32[768,3584]{1,0:T(8,128)} %fusion.23, f32[768,3584]{1,0:T(8,128)} %fusion.22, bf16[768,512]{0,1:T(8,128)(2,1)S(1)} %copy-done.5, bf16[2,3584,512]{2,1,0:T(8,128)(2,1)} %bitcast_dynamic-update-slice_fusion), kind=kOutput, calls=%fused_computation.3 | convolution fusion | flops 2829582336 | bytes 42991616 | tf_op jit(solution)/shard_map/dot_general | solution.py:36
  324.5 0.6 select_convert_fusion
  325.1 0.2 reshape.240
  325.3 3.0 pad_maximum_fusion.1
  328.4 74.9 %all_to_all.10 = bf16[32,24,3712]{2,1,0:T(8,128)(2,1)S(1)} all-to-all(bf16[32,24,3712]{2,1,0:T(8,128)(2,1)S(1)} %pad_maximum_fusion.1), channel_id=1, replica_groups=mesh['expert'=32,'dp'=4] {'expert'}, dimensions={0} | all-to-all | bytes 11403264 | tf_op jit(solution)/shard_map/all_to_all | solution.py:122
  403.3 2.5 copy-done.4
  405.9 0.1 convert_reduce_fusion.1
  406.0 0.3 select_reduce_fusion
  406.3 0.1 reshape.232
  406.5 0.6 multiply_divide_fusion
  407.1 4.4 %fusion.5 = bf16[64,3584]{1,0:T(8,128)(2,1)} fusion(bf16[768,3712]{1,0:T(8,128)(2,1)} %bitcast.99, bf16[768,64]{0,1:T(8,128)(2,1)S(1)} %convert_reduce_fusion), kind=kOutput, calls=%fused_computation.15 | convolution fusion | flops 352550912 | bytes 6062080 | tf_op jit(solution)/shard_map/dot_general | solution.py:42
  411.5 7.8 %fusion.26 = (bf16[1,256,3584]{2,1,0:T(8,128)(2,1)}, bf16[1,256,3584]{2,1,0:T(8,128)(2,1)}, bf16[1,256,3584]{2,1,0:T(8,128)(2,1)}) fusion(bf16[1,256,3584]{2,1,0:T(8,128)(2,1)} %param.19, bf16[1,128,3584]{2,1,0:T(8,128)(2,1)} %bitcast.100, bf16[1,128,3584]{2,1,0:T(8,128)(2,1)} %bitcast.101, bf16[1,256,3584]{2,1,0:T(8,128)(2,1)} %param.18, ...), kind=kLoop, calls=%fused_computation.40 | loop fusion | flops 23855104 | bytes 12845056 | tf_op jit(solution)/shard_map/convert_element_type | solution.py:144
  (41 shorter events, 0.7 us)
Async XLA Ops:
  23.8 196.0 %all-to-all-start = ((bf16[32,24,7296]{2,1,0:T(8,128)(2,1)}), bf16[32,24,7296]{2,1,0:T(8,128)(2,1)}, u32[]{:S(2)}, u32[]{:S(2)}) async-start(bf16[32,24,7296]{2,1,0:T(8,128)(2,1)} %pad_maximum_fusion), calls=%async_computation | async-start | bytes 22413312 | tf_op jit(solution)/shard_map/all_to_all | solution.py:82
  32.4 196.3 %all-gather.2.cloned.1.call-start = ((), (), s32[]{:S(2)}) async-start(), calls=%async_computation.4 | async-start | bytes 9175040 | tf_op jit(solution)/shard_map/all_gather | solution.py:77
  33.2 378.3 %reduce-scatter.5.cloned.1.call-start = ((), (), s32[]{:S(2)}) async-start(), calls=%async_computation.6 | async-start | bytes 4587520 | tf_op jit(solution)/shard_map/reduce_scatter | solution.py:105
  36.8 72.4 %collective-permute-start.3 = (bf16[1,2,3584,128]{3,2,1,0:T(8,128)(2,1)}, bf16[1,2,3584,128]{3,2,1,0:T(8,128)(2,1)}, u32[]{:S(2)}, u32[]{:S(2)}) collective-permute-start(bf16[1,2,3584,128]{3,2,1,0:T(8,128)(2,1)} %get-tuple-element.53), channel_id=1, source_target_pairs={{0,1},{1,2},{2,3},{3,0},{4,5},{5,6},{6,7},{7,4},{8,9},{9,10},{10,1... | collective-permute-start | bytes 5505032 | tf_op jit(solution)/shard_map/ppermute | solution.py:25
  38.4 144.3 %collective-permute-start.4 = (bf16[1,2,3584,128]{3,2,1,0:T(8,128)(2,1)}, bf16[1,2,3584,128]{3,2,1,0:T(8,128)(2,1)}, u32[]{:S(2)}, u32[]{:S(2)}) collective-permute-start(bf16[1,2,3584,128]{3,2,1,0:T(8,128)(2,1)} %get-tuple-element.53), channel_id=1, source_target_pairs={{0,3},{1,0},{2,1},{3,2},{4,7},{5,4},{6,5},{7,6},{8,11},{9,8},{10,9... | collective-permute-start | bytes 5505032 | tf_op jit(solution)/shard_map/ppermute | solution.py:28
  40.5 138.7 %collective-permute-start = (bf16[1,2,3584,128]{3,2,1,0:T(8,128)(2,1)S(1)}, bf16[1,2,3584,128]{3,2,1,0:T(8,128)(2,1)}, u32[]{:S(2)}, u32[]{:S(2)}) collective-permute-start(bf16[1,2,3584,128]{3,2,1,0:T(8,128)(2,1)S(1)} %get-tuple-element.54), channel_id=1, source_target_pairs={{0,1},{1,2},{2,3},{3,0},{4,5},{5,6},{6,7},{7,4},{8,9},{9,10},{10,1... | collective-permute-start | bytes 5505032 | tf_op jit(solution)/shard_map/ppermute | solution.py:25
  40.5 218.9 %collective-permute-start.1 = (bf16[1,2,3584,128]{3,2,1,0:T(8,128)(2,1)S(1)}, bf16[1,2,3584,128]{3,2,1,0:T(8,128)(2,1)}, u32[]{:S(2)}, u32[]{:S(2)}) collective-permute-start(bf16[1,2,3584,128]{3,2,1,0:T(8,128)(2,1)S(1)} %get-tuple-element.54), channel_id=1, source_target_pairs={{0,3},{1,0},{2,1},{3,2},{4,7},{5,4},{6,5},{7,6},{8,11},{9,8},{10,9... | collective-permute-start | bytes 5505032 | tf_op jit(solution)/shard_map/ppermute | solution.py:28
  43.2 4.1 copy-start
  49.7 135.9 %copy-start.2 = (bf16[2,3584,512]{2,1,0:T(8,128)(2,1)}, bf16[2,3584,512]{2,1,0:T(8,128)(2,1)S(1)}, u32[]{:S(2)}) copy-start(bf16[2,3584,512]{2,1,0:T(8,128)(2,1)S(1)} %bitcast_dynamic-update-slice_fusion.7) | copy-start | bytes 22020100
  109.2 109.2 %collective-permute-start.5 = (bf16[1,2,3584,128]{3,2,1,0:T(8,128)(2,1)}, bf16[1,2,3584,128]{3,2,1,0:T(8,128)(2,1)S(1)}, u32[]{:S(2)}, u32[]{:S(2)}) collective-permute-start(bf16[1,2,3584,128]{3,2,1,0:T(8,128)(2,1)} %collective-permute-done.3), channel_id=1, source_target_pairs={{0,1},{1,2},{2,3},{3,0},{4,5},{5,6},{6,7},{7,4},{8,9},{9,10},{10,1... | collective-permute-start | bytes 5505032 | tf_op jit(solution)/shard_map/ppermute | solution.py:25
  179.2 83.2 %collective-permute-start.2 = (bf16[1,2,3584,128]{3,2,1,0:T(8,128)(2,1)}, bf16[1,2,3584,128]{3,2,1,0:T(8,128)(2,1)}, u32[]{:S(2)}, u32[]{:S(2)}) collective-permute-start(bf16[1,2,3584,128]{3,2,1,0:T(8,128)(2,1)} %collective-permute-done), channel_id=1, source_target_pairs={{0,1},{1,2},{2,3},{3,0},{4,5},{5,6},{6,7},{7,4},{8,9},{9,10},{10,1... | collective-permute-start | bytes 5505032 | tf_op jit(solution)/shard_map/ppermute | solution.py:25
  238.6 1.4 copy-start.8
  256.2 155.3 %reduce-scatter.3.cloned.1.call-start = ((), (), s32[]{:S(2)}) async-start(), calls=%async_computation.5 | async-start | bytes 4587520 | tf_op jit(solution)/shard_map/reduce_scatter | solution.py:105
  265.3 7.6 %copy-start.3 = (bf16[2,3584,512]{2,1,0:T(8,128)(2,1)S(1)}, bf16[2,3584,512]{2,1,0:T(8,128)(2,1)}, u32[]{:S(2)}) copy-start(bf16[2,3584,512]{2,1,0:T(8,128)(2,1)} %bitcast_dynamic-update-slice_fusion.4) | copy-start | bytes 22020100
  285.4 5.8 %copy-start.7 = (bf16[768,512]{0,1:T(8,128)(2,1)S(1)}, bf16[768,512]{0,1:T(8,128)(2,1)}, u32[]{:S(2)}) copy-start(bf16[768,512]{0,1:T(8,128)(2,1)} %get-tuple-element.49) | copy-start | bytes 2359300
  306.7 1.1 copy-start.5
  328.4 78.1 %copy-start.6 = (f32[64,8]{0,1:T(8,128)S(1)}, f32[64,8]{0,1:T(8,128)}, u32[]{:S(2)}) copy-start(f32[64,8]{0,1:T(8,128)} %param.15) | copy-start | bytes 6148
  403.3 2.6 copy-start.4
  403.3 8.2 %copy-start.1 = (bf16[1,256,3584]{2,1,0:T(8,128)(2,1)S(1)}, bf16[1,256,3584]{2,1,0:T(8,128)(2,1)}, u32[]{:S(2)}) copy-start(bf16[1,256,3584]{2,1,0:T(8,128)(2,1)} %param.17) | copy-start | bytes 5505028
Sparse Core Ops, SparseCore 0:
  34.9 135.6 all-gather.1
  256.3 43.7 reduce-scatter.4
  306.8 43.7 reduce-scatter.2
